TPU v7x, 32 devices: a whole 2x2x4 slice. The times are simulated.
32 devices in a mesh: parts: 2 (over y), tm: 4 (over x, core), cols: 4 (over z).
Axes of the slice: x: 2, y: 2, z: 4, core: 2. Of those that a mesh axis runs over, the one named last changes fastest.
Arguments:
- noise: float32 [16, 1024, 1024], P(('parts', 'tm'), None, 'cols'), parts along dimension 0, may hold values from -6 to 6
- inv_diag: float32 [16, 1024, 1024], P(('parts', 'tm'), None, 'cols'), parts along dimension 0, may hold values from -2 to 2, as said below
- coupling: float32 [16, 1024, 1024], P(('parts', 'tm'), None, 'cols'), parts along dimension 0, may hold values from -1 to 1, as said below
- order: int32 [1024], replicated, may hold values from 0 to 1023, each once
Outputs:
- sample: float32 [16, 1024, 1024], P(('parts', 'tm'), None, 'cols'), parts along dimension 0
There are 2 independent parts, one for each index of `parts`. A program takes and returns all parts, laid end to end along the dimension named above; an argument that names none is the same for every part. Nothing has to cross between parts.
Inputs may be any that keep to these rules, and one draw needn't show every extreme that they name: `order`: each of 0 to 1023 appears once. `inv_diag`: diagonal entries lie between 0.5 and 2, off-diagonal entries are small in magnitude. `coupling`: diagonal entries lie between 0.5 and 0.97, off-diagonal entries are small in magnitude.
All inputs are finite; a program needn't handle non-finite values.
Results may differ from a plain program's by a relative error of at most 0.00013.
Values sent between devices are 32-bit elements; how exact they have to be, the bound alone decides.
No kernel may reach another device: no remote copies, remote signals or barrier semaphores. Data moves between devices by JAX's collectives and lax.ppermute only.
A program may use at most 128 MiB of HBM per device.

v0:
```python
import jax
import jax.numpy as jnp
from jax import lax
from jax.sharding import PartitionSpec as P

low = jnp.bfloat16


def shifted(block, axis, distance):
    devices = range(lax.axis_size(axis))
    route = [(i - distance, i) for i in devices if i - distance in devices]
    return lax.ppermute(block, axis, route)


def split(value, count):
    parts = []
    rest = value
    for index in range(count):
        kept = lax.reduce_precision(rest, exponent_bits=8, mantissa_bits=7)
        parts.append(kept.astype(low))
        if index < count - 1:
            rest = rest - kept
    return parts


def bdot(left, right):
    return jnp.dot(left, right, preferred_element_type=jnp.float32)


def apply(matrix_parts, operand):
    high, small = matrix_parts
    operand_high, operand_small = split(operand, 2)
    return bdot(high, operand_high) + (bdot(high, operand_small) + bdot(small, operand_high))


def shards(noise, inv_diag, coupling, order):
    block_count = noise.shape[0]
    node_count = noise.shape[1]
    sample_count = noise.shape[2]
    pieces = 2 if sample_count % 256 == 0 else 1
    width = sample_count // pieces
    inv_full = lax.all_gather(inv_diag, "cols", axis=2, tiled=True)
    coupling_parts = [
        split(lax.all_gather(coupling[block], "cols", axis=1, tiled=True), 2)
        for block in range(block_count)
    ]
    driven = [apply(split(inv_full[block], 2), noise[block]) for block in range(block_count)]
    driven_pieces = [
        [driven[block][:, p * width : (p + 1) * width] for p in range(pieces)]
        for block in range(block_count)
    ]

    def chain(entering, piece, skip_last):
        carried = entering
        results = [None] * block_count
        for block in range(block_count - 1, -1, -1):
            if skip_last and block == block_count - 1:
                carried = driven_pieces[block][piece]
            else:
                carried = driven_pieces[block][piece] + apply(coupling_parts[block], carried)
            results[block] = carried
        return results

    first = [shifted(chain(None, p, True)[0], "tm", -1) for p in range(pieces)]

    def relay_step(step, entering):
        return [shifted(chain(entering[p], p, False)[0], "tm", -1) for p in range(pieces)]

    entering = lax.fori_loop(0, lax.axis_size("tm") - 2, relay_step, first)
    finals = [chain(entering[p], p, False) for p in range(pieces)]
    selector = (order[:, None] == jnp.arange(node_count, dtype=order.dtype)[None, :]).astype(low)
    outputs = []
    for block in range(block_count):
        field = jnp.concatenate([finals[p][block] for p in range(pieces)], axis=1)
        top, middle, bottom = split(field, 3)
        outputs.append(bdot(selector, top) + (bdot(selector, middle) + bdot(selector, bottom)))
    return jnp.stack(outputs, axis=0)


def solution(mesh):
    return jax.shard_map(
        shards,
        mesh=mesh,
        in_specs=(
            P(("parts", "tm"), None, "cols"),
            P(("parts", "tm"), None, "cols"),
            P(("parts", "tm"), None, "cols"),
            P(),
        ),
        out_specs=P(("parts", "tm"), None, "cols"),
        check_vma=False,
    )
```

profile of v0, /device:TPU:1, one launch (start us, length us, event | category | flops | bytes accessed | tf_op | source)
XLA Modules:
  0.0 439.5 jit_solution(6839977181822519246)
XLA Ops:
  6.5 3.0 fusion.150
  11.0 81.5 %all-gather.8.cloned.1.call-done = f32[1,1024,1024]{2,1,0:T(8,128)} async-done(((f32[1,1024,256]{2,1,0:T(8,128)}), f32[1,1024,1024]{2,1,0:T(8,128)}) %all-gather.8.cloned.1.call-update) | async-done | bytes 4194320 | tf_op jit(solution)/shard_map/all_gather | solution.py:44
  92.6 4.4 %reduce-precision_convert_fusion.13 = (bf16[1024,1024]{1,0:T(8,128)(2,1)S(1)}, bf16[1024,1024]{1,0:T(8,128)(2,1)}) fusion(f32[1,1024,1024]{2,1,0:T(8,128)} %all-gather.8.cloned.1.call-done), kind=kLoop, calls=%fused_computation.43 | loop fusion | flops 5242880 | bytes 8388608 | tf_op jit(solution)/shard_map/convert_element_type | solution.py:20
  97.0 76.5 %all-gather.10.cloned.1.call-done = f32[1,1024,1024]{2,1,0:T(8,128)} async-done(((f32[1,1024,256]{2,1,0:T(8,128)}), f32[1,1024,1024]{2,1,0:T(8,128)}) %all-gather.10.cloned.1.call-update) | async-done | bytes 4194320 | tf_op jit(solution)/shard_map/all_gather | solution.py:44
  173.5 5.0 %reduce-precision_convert_fusion.12 = (bf16[1024,1024]{1,0:T(8,128)(2,1)}, bf16[1024,1024]{1,0:T(8,128)(2,1)}) fusion(f32[1,1024,1024]{2,1,0:T(8,128)} %all-gather.10.cloned.1.call-done), kind=kLoop, calls=%fused_computation.41 | loop fusion | flops 5242880 | bytes 8388608 | tf_op jit(solution)/shard_map/convert_element_type | solution.py:20
  178.5 144.9 %all-gather.6.cloned.1.call-done = f32[2,1024,1024]{2,1,0:T(8,128)} async-done(((f32[2,1024,256]{2,1,0:T(8,128)}), f32[2,1024,1024]{2,1,0:T(8,128)}) %all-gather.6.cloned.1.call-update) | async-done | bytes 8388624 | tf_op jit(solution)/shard_map/all_gather | solution.py:42
  323.4 3.4 fusion.47
  326.9 3.8 fusion.97
  334.1 0.8 fusion.75
  334.9 0.8 fusion.72
  338.1 1.7 fusion.74
  339.8 1.7 fusion.71
  341.5 2.4 collective-permute-start.2
  343.8 2.1 collective-permute-start.3
  345.9 1.1 fusion.152
  347.0 2.0 copy.10
  349.0 2.0 copy.9
  351.1 2.3 fusion.151
  353.4 4.4 %collective-permute-done.3 = f32[1024,128]{0,1:T(8,128)S(1)} collective-permute-done((f32[1024,128]{0,1:T(8,128)}, f32[1024,128]{0,1:T(8,128)S(1)}, u32[]{:S(2)}, u32[]{:S(2)}) %collective-permute-start.3) | collective-permute-done | bytes 524320 | tf_op jit(solution)/shard_map/ppermute | solution.py:12
  357.8 54.2 %while.12 = (s32[]{:T(128)}, f32[1024,128]{0,1:T(8,128)S(1)}, f32[1024,128]{0,1:T(8,128)S(1)}, bf16[1024,1024]{1,0:T(8,128)(2,1)}, bf16[1024,1024]{1,0:T(8,128)(...) while((s32[]{:T(128)}, f32[1024,128]{0,1:T(8,128)S(1)}, ...), condition=%wide.region_1.0_spmd, body=%wide.region_0.0_spmd.sunk | while | flops 3226992640 | bytes 81789320 | solution.py:69
  357.8 2.5 fusion.228
  364.5 1.7 fusion.232
  366.2 1.9 collective-permute-start
  372.5 1.7 fusion.238
  374.2 1.9 collective-permute-start.1
  376.9 8.0 %collective-permute-done.1 = f32[1024,128]{0,1:T(8,128)S(1)} collective-permute-done((f32[1024,128]{0,1:T(8,128)}, f32[1024,128]{0,1:T(8,128)S(1)}, u32[]{:S(2)}, u32[]{:S(2)}) %collective-permute-start.1) | collective-permute-done | bytes 524320 | tf_op jit(solution)/shard_map/while/body/eval_jaxpr/ppermute | solution.py:12
  384.9 2.5 fusion.228
  391.7 1.7 fusion.232
  393.3 1.9 collective-permute-start
  399.7 1.7 fusion.238
  401.3 1.9 collective-permute-start.1
  404.0 8.0 %collective-permute-done.1 = f32[1024,128]{0,1:T(8,128)S(1)} collective-permute-done((f32[1024,128]{0,1:T(8,128)}, f32[1024,128]{0,1:T(8,128)S(1)}, u32[]{:S(2)}, u32[]{:S(2)}) %collective-permute-start.1) | collective-permute-done | bytes 524320 | tf_op jit(solution)/shard_map/while/body/eval_jaxpr/ppermute | solution.py:12
  412.0 2.6 fusion.136
  416.2 0.8 fusion.78
  417.4 0.8 fusion.77
  418.3 0.8 fusion.84
  419.1 0.8 fusion.83
  422.4 0.8 fusion.81
  423.6 0.8 fusion.80
  424.4 0.8 fusion.87
  425.3 0.8 fusion.86
  426.2 0.9 fusion.40
  427.0 0.9 fusion.43
  427.9 0.9 fusion.62
  428.8 0.9 fusion.61
  429.7 0.9 fusion.65
  430.6 0.9 fusion.64
  431.5 1.5 pad_maximum_fusion
  (86 shorter events, 30.6 us)
Async XLA Ops:
  6.5 86.0 %all-gather.8.cloned.1.call-start = ((), (), s32[]{:S(2)}) async-start(), calls=%async_computation.1 | async-start | bytes 5242880 | tf_op jit(solution)/shard_map/all_gather | solution.py:44
  9.6 163.9 %all-gather.10.cloned.1.call-start = ((), (), s32[]{:S(2)}) async-start(), calls=%async_computation.2 | async-start | bytes 5242880 | tf_op jit(solution)/shard_map/all_gather | solution.py:44
  10.3 313.1 %all-gather.6.cloned.1.call-start = ((), (), s32[]{:S(2)}) async-start(), calls=%async_computation | async-start | bytes 10485760 | tf_op jit(solution)/shard_map/all_gather | solution.py:42
  323.4 7.2 %copy-start.7 = (f32[2,1024,1024]{2,1,0:T(8,128)S(1)}, f32[2,1024,1024]{2,1,0:T(8,128)}, u32[]{:S(2)}) copy-start(f32[2,1024,1024]{2,1,0:T(8,128)} %all-gather.6.cloned.1.call-done) | copy-start | bytes 25165828
  326.8 4.0 copy-start.14
  330.8 1.6 copy-start.2
  331.6 14.3 %copy-start.8 = (f32[1024,256]{0,1:T(8,128)}, f32[1024,256]{0,1:T(8,128)S(1)}, u32[]{:S(2)}) copy-start(f32[1024,256]{0,1:T(8,128)S(1)} %fusion.69) | copy-start | bytes 3145732
  338.1 1.7 copy-start.15
  341.5 11.9 %collective-permute-start.2 = (f32[1024,128]{0,1:T(8,128)}, f32[1024,128]{0,1:T(8,128)S(1)}, u32[]{:S(2)}, u32[]{:S(2)}) collective-permute-start(f32[1024,128]{0,1:T(8,128)} %fusion.71), channel_id=1, source_target_pairs={{4,0},{8,4},{12,8},{5,1},{9,5},{13,9},{6,2},{10,6},{14,10},{7,3},{... | collective-permute-start | bytes 1572872 | tf_op jit(solution)/shard_map/ppermute | solution.py:12
  343.8 14.0 %collective-permute-start.3 = (f32[1024,128]{0,1:T(8,128)}, f32[1024,128]{0,1:T(8,128)S(1)}, u32[]{:S(2)}, u32[]{:S(2)}) collective-permute-start(f32[1024,128]{0,1:T(8,128)} %fusion.74), channel_id=1, source_target_pairs={{4,0},{8,4},{12,8},{5,1},{9,5},{13,9},{6,2},{10,6},{14,10},{7,3},{... | collective-permute-start | bytes 1572872 | tf_op jit(solution)/shard_map/ppermute | solution.py:12
  357.8 2.5 copy-start
  360.2 1.0 copy-start.11
  362.9 1.6 copy-start.3
  362.9 1.7 copy-start.13
  364.5 3.6 copy-start.5
  366.2 10.7 %collective-permute-start = (f32[1024,128]{0,1:T(8,128)}, f32[1024,128]{0,1:T(8,128)S(1)}, u32[]{:S(2)}, u32[]{:S(2)}) collective-permute-start(f32[1024,128]{0,1:T(8,128)} %fusion.232), channel_id=1, source_target_pairs={{4,0},{8,4},{12,8},{5,1},{9,5},{13,9},{6,2},{10,6},{14,10},{7,3},{... | collective-permute-start | bytes 1572872 | tf_op jit(solution)/shard_map/while/body/eval_jaxpr/ppermute | solution.py:12
  368.8 1.0 copy-start.10
  371.5 1.0 copy-start.12
  374.2 10.7 %collective-permute-start.1 = (f32[1024,128]{0,1:T(8,128)}, f32[1024,128]{0,1:T(8,128)S(1)}, u32[]{:S(2)}, u32[]{:S(2)}) collective-permute-start(f32[1024,128]{0,1:T(8,128)} %fusion.238), channel_id=1, source_target_pairs={{4,0},{8,4},{12,8},{5,1},{9,5},{13,9},{6,2},{10,6},{14,10},{7,3},{... | collective-permute-start | bytes 1572872 | tf_op jit(solution)/shard_map/while/body/eval_jaxpr/ppermute | solution.py:12
  384.9 2.5 copy-start
  387.4 1.0 copy-start.11
  390.0 1.6 copy-start.3
  390.0 1.7 copy-start.13
  391.6 3.6 copy-start.5
  393.3 10.7 %collective-permute-start = (f32[1024,128]{0,1:T(8,128)}, f32[1024,128]{0,1:T(8,128)S(1)}, u32[]{:S(2)}, u32[]{:S(2)}) collective-permute-start(f32[1024,128]{0,1:T(8,128)} %fusion.232), channel_id=1, source_target_pairs={{4,0},{8,4},{12,8},{5,1},{9,5},{13,9},{6,2},{10,6},{14,10},{7,3},{... | collective-permute-start | bytes 1572872 | tf_op jit(solution)/shard_map/while/body/eval_jaxpr/ppermute | solution.py:12
  396.0 1.0 copy-start.10
  398.6 1.0 copy-start.12
  401.3 10.7 %collective-permute-start.1 = (f32[1024,128]{0,1:T(8,128)}, f32[1024,128]{0,1:T(8,128)S(1)}, u32[]{:S(2)}, u32[]{:S(2)}) collective-permute-start(f32[1024,128]{0,1:T(8,128)} %fusion.238), channel_id=1, source_target_pairs={{4,0},{8,4},{12,8},{5,1},{9,5},{13,9},{6,2},{10,6},{14,10},{7,3},{... | collective-permute-start | bytes 1572872 | tf_op jit(solution)/shard_map/while/body/eval_jaxpr/ppermute | solution.py:12
  412.0 2.6 copy-start.6
  414.6 1.6 copy-start.1
  416.2 1.2 copy-start.9
  419.1 1.6 copy-start.4
  422.4 1.2 copy-start.16
  425.3 0.9 copy-start.17
Sparse Core Ops, SparseCore 0:
  9.7 82.8 all-gather.7
  94.1 79.2 all-gather.9
  175.0 148.3 all-gather.5
where the time goes:
time: 440 us; the launch traced here: 439 us
  waiting for transfers between devices  326 us (74%)
  matrix products  59.5 us (14%)
  local copies, waits for them, and re-layouts  16.8 us (4%)
  between operations  13.4 us (3%)
  starting transfers between devices  12.2 us (3%)
  other arithmetic  10.9 us (2%)
    all_gather x2, waiting for transfers between devices, shards(): lax.all_gather(coupling[block], 'cols', axis=1, tiled=True)  158 us
    all_gather x1, waiting for transfers between devices, shards(): inv_full = lax.all_gather(inv_diag, 'cols', axis=2, tiled=True)  145 us
    dot_general x54, matrix products, bdot(): return jnp.dot(left, right, preferred_element_type=jnp.float32)  59.5 us
    ppermute x6, waiting for transfers between devices, shifted(): return lax.ppermute(block, axis, route)  22 us
    ppermute x6, starting transfers between devices, shifted(): return lax.ppermute(block, axis, route)  12.1 us
    convert_element_type x2, other arithmetic, split(): parts.append(kept.astype(low))  9.48 us
  transfers between devices with their start and end apart: 9, of which 8 were waited for; matrix products, arithmetic and copies ran while one was open for 6% of the time, Pallas kernels for 0%

commit v1 on v0

--- a/solution.py
+++ b/solution.py
@@ -4,6 +4,12 @@
 from jax.sharding import PartitionSpec as P
 
 low = jnp.bfloat16
+
+
+def in_order(tiles, dim):
+    lengths = list(tiles.shape[1:])
+    lengths[dim] *= tiles.shape[0]
+    return jnp.moveaxis(tiles, 0, dim).reshape(lengths)
 
 
 def shifted(block, axis, distance):
@@ -39,7 +45,14 @@
     sample_count = noise.shape[2]
     pieces = 2 if sample_count % 256 == 0 else 1
     width = sample_count // pieces
-    inv_full = lax.all_gather(inv_diag, "cols", axis=2, tiled=True)
+    size = lax.axis_size("cols")
+    ahead = [(i_2, (i_2 + 1) % size) for i_2 in range(size)]
+    blocks = [inv_diag]
+    while len(blocks) < size:
+        blocks.append(lax.ppermute(blocks[-1], "cols", ahead))
+    mine = lax.axis_index("cols")
+    blocks = jnp.stack(blocks)[(mine - jnp.arange(size)) % size]
+    inv_full = in_order(blocks, 2)
     coupling_parts = [
         split(lax.all_gather(coupling[block], "cols", axis=1, tiled=True), 2)
         for block in range(block_count)

time: 440 us -> 442 us (level)
  the two profiles are of different devices: /device:TPU:1 before, /device:TPU:17 now
where the time goes in v1:
time: 442 us; the launch traced here: 441 us
  waiting for transfers between devices  277 us (63%)
  matrix products  57.8 us (13%)
  local copies, waits for them, and re-layouts  41.5 us (9%)
  starting transfers between devices  28.3 us (6%)
  other arithmetic  22.3 us (5%)
  between operations  13.8 us (3%)
    ppermute x3, waiting for transfers between devices, shards(): blocks.append(lax.ppermute(blocks[-1], 'cols', ahead))  259 us
    dot_general x54, matrix products, bdot(): return jnp.dot(left, right, preferred_element_type=jnp.float32)  57.8 us
    ppermute x6, starting transfers between devices, shifted(): return lax.ppermute(block, axis, route)  24.6 us
    ppermute x6, waiting for transfers between devices, shifted(): return lax.ppermute(block, axis, route)  17.6 us
    convert_element_type x3, other arithmetic, split(): parts.append(kept.astype(low))  15.2 us
    convert_element_type x4, local copies, waits for them, and re-layouts, split(): parts.append(kept.astype(low))  13.4 us
  transfers between devices with their start and end apart: 11, of which 7 were waited for; matrix products, arithmetic and copies ran while one was open for 17% of the time, Pallas kernels for 0%

profile of v1, /device:TPU:17, one launch (start us, length us, event | category | flops | bytes accessed | tf_op | source)
XLA Modules:
  0.0 440.6 jit_solution(10559998182430874481)
XLA Ops:
  6.5 3.2 fusion.140
  9.8 1.3 collective-permute-start.2
  11.2 112.7 %collective-permute-done.2 = f32[2,1024,256]{2,1,0:T(8,128)S(1)} collective-permute-done((f32[2,1024,256]{2,1,0:T(8,128)S(1)}, f32[2,1024,256]{2,1,0:T(8,128)S(1)}, u32[]{:S(2)}, u32[]{:S(2)}) %collective-permute-start.2) | collective-permute-done | bytes 2097184 | tf_op jit(solution)/shard_map/ppermute | solution.py:52
  123.9 1.3 copy-done.21
  125.2 1.2 collective-permute-start.3
  126.4 44.6 %collective-permute-done.3 = f32[2,1024,256]{2,1,0:T(8,128)} collective-permute-done((f32[2,1024,256]{2,1,0:T(8,128)S(1)}, f32[2,1024,256]{2,1,0:T(8,128)}, u32[]{:S(2)}, u32[]{:S(2)}) %collective-permute-start.3) | collective-permute-done | bytes 2097184 | tf_op jit(solution)/shard_map/ppermute | solution.py:52
  171.0 1.1 collective-permute-start.4
  172.1 101.7 %collective-permute-done.4 = f32[2,1024,256]{2,1,0:T(8,128)} collective-permute-done((f32[2,1024,256]{2,1,0:T(8,128)}, f32[2,1024,256]{2,1,0:T(8,128)}, u32[]{:S(2)}, u32[]{:S(2)}) %collective-permute-start.4) | collective-permute-done | bytes 2097184 | tf_op jit(solution)/shard_map/ppermute | solution.py:52
  273.9 5.6 %pad_maximum_fusion = f32[4,2,1024,256]{3,2,1,0:T(8,128)} fusion(f32[1,2,1024,256]{3,2,1,0:T(8,128)} %bitcast.7, f32[1,2,1024,256]{3,2,1,0:T(8,128)} %bitcast.6, f32[1,2,1024,256]{3,2,1,0:T(8,128)} %bitcast.195, f32[1,2,1024,256]{3,2,1,0:T(8,128)S(1)} %bitcast.194), kind=kLoop, calls=%fused_computation.41 | loop fusion | flops 6291456 | bytes 16777216 | tf_op jit(solution)/shard_map/stack | solution.py:54
  279.4 7.7 %gather_fusion = f32[4,2,1024,256]{3,2,1,0:T(8,128)} fusion(f32[4,2,1024,256]{3,2,1,0:T(8,128)} %pad_maximum_fusion, s32[1024]{0:T(1024)S(1)} %pad_clamp_fusion), kind=kCustom, calls=%fused_computation | custom fusion | bytes 16777232 | tf_op jit(solution)/shard_map/gather | solution.py:54
  287.2 7.2 %fusion.33 = (bf16[1,1024,4,256]{3,1,0,2:T(8,128)(2,1)}, bf16[1,1024,4,256]{3,1,0,2:T(8,128)(2,1)}, bf16[1,1024,4,256]{3,1,0,2:T(8,128)(2,1)}, bf16[1,1024,4,256]{3,1,0,2:T(8,128)(2,1)S(1)}) fusion(f32[2,1024,4,256]{3,1,0,2:T(8,128)} %bitcast.187), kind=kLoop, calls=%fused_computation.51 | loop fusion | flops 10485760 | bytes 16777216 | tf_op jit(solution)/shard_map/convert_element_type | solution.py:26
  294.3 4.0 copy.21
  298.3 4.0 copy.22
  302.3 2.5 copy.19
  304.8 3.0 copy.20
  307.8 2.8 fusion.101
  313.3 1.0 fusion.142
  314.4 1.3 copy-done.17
  317.2 1.8 fusion.59
  319.0 2.9 reduce-precision_convert_fusion.13
  324.0 1.6 fusion.64
  325.6 15.1 %collective-permute-start.6 = (f32[1024,128]{0,1:T(8,128)}, f32[1024,128]{0,1:T(8,128)S(1)}, u32[]{:S(2)}, u32[]{:S(2)}) collective-permute-start(f32[1024,128]{0,1:T(8,128)} %fusion.64), channel_id=1, source_target_pairs={{4,0},{8,4},{12,8},{5,1},{9,5},{13,9},{6,2},{10,6},{14,10},{7,3},{... | collective-permute-start | bytes 1572872 | tf_op jit(solution)/shard_map/ppermute | solution.py:18
  340.7 1.9 fusion.120
  343.5 1.6 fusion.61
  345.1 1.9 collective-permute-start.5
  347.0 1.1 fusion.141
  348.1 2.0 copy.25
  350.2 2.1 copy.26
  352.2 5.1 %reduce-precision_convert_fusion.12 = (bf16[1024,1024]{1,0:T(8,128)(2,1)}, bf16[1024,1024]{1,0:T(8,128)(2,1)}) fusion(f32[1,1024,1024]{2,1,0:T(8,128)} %all-gather.7.cloned.1.call-done), kind=kLoop, calls=%fused_computation.43 | loop fusion | flops 5242880 | bytes 8388608 | tf_op jit(solution)/shard_map/convert_element_type | solution.py:26
  357.4 55.5 %while.12 = (s32[]{:T(128)}, f32[1024,128]{0,1:T(8,128)S(1)}, f32[1024,128]{0,1:T(8,128)S(1)}, bf16[1024,1024]{1,0:T(8,128)(2,1)}, bf16[1024,1024]{1,0:T(8,128)(...) while((s32[]{:T(128)}, f32[1024,128]{0,1:T(8,128)S(1)}, ...), condition=%wide.region_1.2_spmd, body=%wide.region_0.1_spmd.sunk | while | flops 3226992640 | bytes 81789320 | solution.py:82
  357.4 2.5 fusion.229
  364.7 1.7 fusion.234
  366.4 1.9 collective-permute-start.1
  372.7 1.6 fusion.228
  374.4 1.9 collective-permute-start
  377.1 8.0 %collective-permute-done = f32[1024,128]{0,1:T(8,128)S(1)} collective-permute-done((f32[1024,128]{0,1:T(8,128)}, f32[1024,128]{0,1:T(8,128)S(1)}, u32[]{:S(2)}, u32[]{:S(2)}) %collective-permute-start) | collective-permute-done | bytes 524320 | tf_op jit(solution)/shard_map/while/body/eval_jaxpr/ppermute | solution.py:18
  385.1 2.4 fusion.229
  392.5 1.7 fusion.234
  394.1 1.9 collective-permute-start.1
  400.5 1.6 fusion.228
  402.1 1.9 collective-permute-start
  404.8 8.0 %collective-permute-done = f32[1024,128]{0,1:T(8,128)S(1)} collective-permute-done((f32[1024,128]{0,1:T(8,128)}, f32[1024,128]{0,1:T(8,128)S(1)}, u32[]{:S(2)}, u32[]{:S(2)}) %collective-permute-start) | collective-permute-done | bytes 524320 | tf_op jit(solution)/shard_map/while/body/eval_jaxpr/ppermute | solution.py:18
  412.8 2.6 fusion.122
  428.7 0.9 fusion.54
  429.6 0.9 fusion.53
  430.5 0.9 fusion.57
  431.4 0.9 fusion.56
  432.3 1.5 pad_maximum_fusion.1
  (108 shorter events, 40.5 us)
Async XLA Ops:
  6.5 3.3 copy-start.20
  6.5 312.4 %all-gather.5.cloned.1.call-start = ((), (), s32[]{:S(2)}) async-start(), calls=%async_computation | async-start | bytes 5242880 | tf_op jit(solution)/shard_map/all_gather | solution.py:57
  9.8 342.5 %all-gather.7.cloned.1.call-start = ((), (), s32[]{:S(2)}) async-start(), calls=%async_computation.1 | async-start | bytes 5242880 | tf_op jit(solution)/shard_map/all_gather | solution.py:57
  9.8 114.1 %collective-permute-start.2 = (f32[2,1024,256]{2,1,0:T(8,128)S(1)}, f32[2,1024,256]{2,1,0:T(8,128)S(1)}, u32[]{:S(2)}, u32[]{:S(2)}) collective-permute-start(f32[2,1024,256]{2,1,0:T(8,128)S(1)} %copy-done.20), channel_id=1, source_target_pairs={{0,1},{1,2},{2,3},{3,0},{4,5},{5,6},{6,7},{7,4},{8,9},{9,10},{10,1... | collective-permute-start | bytes 6291464 | tf_op jit(solution)/shard_map/ppermute | solution.py:52
  123.9 1.3 copy-start.21
  125.2 45.8 %collective-permute-start.3 = (f32[2,1024,256]{2,1,0:T(8,128)S(1)}, f32[2,1024,256]{2,1,0:T(8,128)}, u32[]{:S(2)}, u32[]{:S(2)}) collective-permute-start(f32[2,1024,256]{2,1,0:T(8,128)S(1)} %collective-permute-done.2), channel_id=1, source_target_pairs={{0,1},{1,2},{2,3},{3,0},{4,5},{5,6},{6,7},{7,4},{8,9},{9,10},{10,1... | collective-permute-start | bytes 6291464 | tf_op jit(solution)/shard_map/ppermute | solution.py:52
  171.0 102.9 %collective-permute-start.4 = (f32[2,1024,256]{2,1,0:T(8,128)}, f32[2,1024,256]{2,1,0:T(8,128)}, u32[]{:S(2)}, u32[]{:S(2)}) collective-permute-start(f32[2,1024,256]{2,1,0:T(8,128)} %collective-permute-done.3), channel_id=1, source_target_pairs={{0,1},{1,2},{2,3},{3,0},{4,5},{5,6},{6,7},{7,4},{8,9},{9,10},{10,1... | collective-permute-start | bytes 6291464 | tf_op jit(solution)/shard_map/ppermute | solution.py:52
  307.8 2.8 copy-start.18
  307.8 3.2 copy-start.19
  310.9 1.6 copy-start.16
  313.3 10.3 %copy-start.7 = (f32[1024,256]{0,1:T(8,128)}, f32[1024,256]{0,1:T(8,128)S(1)}, u32[]{:S(2)}) copy-start(f32[1024,256]{0,1:T(8,128)S(1)} %fusion.58) | copy-start | bytes 3145732
  313.3 2.3 copy-start.17
  321.9 18.8 %copy-start.2 = (bf16[1024,1024]{1,0:T(8,128)(2,1)}, bf16[1024,1024]{1,0:T(8,128)(2,1)S(1)}, u32[]{:S(2)}) copy-start(bf16[1024,1024]{1,0:T(8,128)(2,1)S(1)} %get-tuple-element.208) | copy-start | bytes 6291460
  322.8 1.2 copy-start.10
  325.6 17.0 %copy-start.8 = (f32[1024,256]{0,1:T(8,128)S(1)}, f32[1024,256]{0,1:T(8,128)}, u32[]{:S(2)}) copy-start(f32[1024,256]{0,1:T(8,128)} %copy-done.7) | copy-start | bytes 3145732
  325.6 31.7 %collective-permute-start.6 = (f32[1024,128]{0,1:T(8,128)}, f32[1024,128]{0,1:T(8,128)S(1)}, u32[]{:S(2)}, u32[]{:S(2)}) collective-permute-start(f32[1024,128]{0,1:T(8,128)} %fusion.64), channel_id=1, source_target_pairs={{4,0},{8,4},{12,8},{5,1},{9,5},{13,9},{6,2},{10,6},{14,10},{7,3},{... | collective-permute-start | bytes 1572872 | tf_op jit(solution)/shard_map/ppermute | solution.py:18
  345.1 12.2 %collective-permute-start.5 = (f32[1024,128]{0,1:T(8,128)}, f32[1024,128]{0,1:T(8,128)S(1)}, u32[]{:S(2)}, u32[]{:S(2)}) collective-permute-start(f32[1024,128]{0,1:T(8,128)} %fusion.61), channel_id=1, source_target_pairs={{4,0},{8,4},{12,8},{5,1},{9,5},{13,9},{6,2},{10,6},{14,10},{7,3},{... | collective-permute-start | bytes 1572872 | tf_op jit(solution)/shard_map/ppermute | solution.py:18
  357.4 2.5 copy-start.5
  359.8 1.6 copy-start
  359.8 1.7 copy-start.13
  363.1 1.6 copy-start.3
  363.1 1.7 copy-start.14
  366.4 10.7 %collective-permute-start.1 = (f32[1024,128]{0,1:T(8,128)}, f32[1024,128]{0,1:T(8,128)S(1)}, u32[]{:S(2)}, u32[]{:S(2)}) collective-permute-start(f32[1024,128]{0,1:T(8,128)} %fusion.234), channel_id=1, source_target_pairs={{4,0},{8,4},{12,8},{5,1},{9,5},{13,9},{6,2},{10,6},{14,10},{7,3},{... | collective-permute-start | bytes 1572872 | tf_op jit(solution)/shard_map/while/body/eval_jaxpr/ppermute | solution.py:18
  369.0 1.0 copy-start.12
  371.7 1.0 copy-start.15
  374.4 10.7 %collective-permute-start = (f32[1024,128]{0,1:T(8,128)}, f32[1024,128]{0,1:T(8,128)S(1)}, u32[]{:S(2)}, u32[]{:S(2)}) collective-permute-start(f32[1024,128]{0,1:T(8,128)} %fusion.228), channel_id=1, source_target_pairs={{4,0},{8,4},{12,8},{5,1},{9,5},{13,9},{6,2},{10,6},{14,10},{7,3},{... | collective-permute-start | bytes 1572872 | tf_op jit(solution)/shard_map/while/body/eval_jaxpr/ppermute | solution.py:18
  385.1 2.5 copy-start.5
  387.5 1.6 copy-start
  387.6 1.7 copy-start.13
  390.8 1.6 copy-start.3
  390.8 1.7 copy-start.14
  394.1 10.7 %collective-permute-start.1 = (f32[1024,128]{0,1:T(8,128)}, f32[1024,128]{0,1:T(8,128)S(1)}, u32[]{:S(2)}, u32[]{:S(2)}) collective-permute-start(f32[1024,128]{0,1:T(8,128)} %fusion.234), channel_id=1, source_target_pairs={{4,0},{8,4},{12,8},{5,1},{9,5},{13,9},{6,2},{10,6},{14,10},{7,3},{... | collective-permute-start | bytes 1572872 | tf_op jit(solution)/shard_map/while/body/eval_jaxpr/ppermute | solution.py:18
  396.8 1.0 copy-start.12
  399.4 1.0 copy-start.15
  402.1 10.7 %collective-permute-start = (f32[1024,128]{0,1:T(8,128)}, f32[1024,128]{0,1:T(8,128)S(1)}, u32[]{:S(2)}, u32[]{:S(2)}) collective-permute-start(f32[1024,128]{0,1:T(8,128)} %fusion.228), channel_id=1, source_target_pairs={{4,0},{8,4},{12,8},{5,1},{9,5},{13,9},{6,2},{10,6},{14,10},{7,3},{... | collective-permute-start | bytes 1572872 | tf_op jit(solution)/shard_map/while/body/eval_jaxpr/ppermute | solution.py:18
  412.8 2.6 copy-start.1
  415.4 1.2 copy-start.9
  416.6 1.6 copy-start.4
  419.1 1.2 copy-start.11
  420.3 1.6 copy-start.6
  426.1 0.9 copy-start.22
Sparse Core Ops, SparseCore 0:
  9.9 115.4 all-gather.4
  172.2 116.3 all-gather.6
